TPU v7x, 256 devices: a whole 4x4x8 slice. The times are simulated.
256 devices in a mesh: tm: 2 (over core), scen: 4 (over x), line: 32 (over z, y).
Axes of the slice: x: 4, y: 4, z: 8, core: 2. Of those that a mesh axis runs over, the one named last changes fastest.
Arguments:
- line_blocks: bfloat16 [64, 128, 1024], P('line'), may hold values from -0.1875 to 0.1875
- binding: int32 [128, 2, 8], P(('scen', 'line'), 'tm'), may hold values from 0 to 63, as said below
- line_weight: float32 [128, 2, 8, 128], P(('scen', 'line'), 'tm'), may hold values from 0.25 to 4
- barrier: float32 [128, 2, 1024], P(('scen', 'line'), 'tm'), may hold values from 0.5 to 4
- gradient: float32 [128, 2, 1024], P(('scen', 'line'), 'tm'), may hold values from -6 to 6
- link_columns: bfloat16 [128, 2, 1024, 128], P(('scen', 'line'), 'tm'), may hold values from -0.5 to 0.5
- ramp_weight: float32 [256], replicated, may hold values from 10 to 200
- link_diag: float32 [128], replicated, may hold values from 0.5 to 5
- link_rhs: float32 [128], replicated, may hold values from -18 to 18
Outputs:
- newton_step: float32 [128, 2, 1024], P(('scen', 'line'), 'tm')
- link_step: float32 [128], replicated
Inputs may be any that keep to these rules, and one draw needn't show every extreme that they name: Block numbers b are held by line device b // 2. Take the list binding[s, t] of one scenario s and period t: exactly one line device holds 2 of its blocks, no line device holds more, and the other blocks are spread as evenly as possible over the other line devices, in a shuffled order. A block may appear more than once.
All inputs are finite; a program needn't handle non-finite values.
Results may differ from a plain program's by a relative error of at most 0.00084.
Values may be sent and summed in bfloat16 or wider, within the bound.
No kernel may reach another device: no remote copies, remote signals or barrier semaphores. Data moves between devices by JAX's collectives and lax.ppermute only.
A program may use at most 128 MiB of HBM per device.

v0:
```python
import jax
import jax.numpy as jnp
from jax import lax
from jax.sharding import PartitionSpec as P

highest = lax.Precision.HIGHEST


def period_hessian(selected, weights, barrier_row, ramp_weight, end_factor):
    order = selected.shape[-1]
    scaled = (weights[:, :, None] * selected.astype(jnp.float32)).astype(jnp.bfloat16)
    flat = selected.reshape(-1, order)
    scaled_flat = scaled.reshape(-1, order)
    hessian = lax.dot_general(
        flat, scaled_flat, (((0,), (0,)), ((), ())), preferred_element_type=jnp.float32
    )
    count = ramp_weight.shape[0]
    extra = jnp.concatenate([end_factor * ramp_weight, jnp.zeros((order - count,), jnp.float32)])
    return hessian + jnp.diag(barrier_row + extra)


def butterfly_sum(value, axes):
    for axis in axes:
        size = lax.axis_size(axis)
        step = 1
        while step < size:
            pairs = [(i, i ^ step) for i in range(size)]
            value = value + lax.ppermute(value, axis, pairs)
            step *= 2
    return value


def trsm(a, b, transpose=False):
    return lax.linalg.triangular_solve(a, b, left_side=True, lower=True, transpose_a=transpose)


def on_device(
    line_blocks,
    binding,
    line_weight,
    barrier,
    gradient,
    link_columns,
    ramp_weight,
    link_diag,
    link_rhs,
):
    block_ids = binding[0, 0]
    order = line_blocks.shape[2]
    count = ramp_weight.shape[0]
    links = link_columns.shape[-1]
    every_block = lax.all_gather(line_blocks, "line", axis=0, tiled=True)
    selected = jnp.take(every_block, block_ids, axis=0)
    shard = lax.axis_index("tm")
    shards = lax.axis_size("tm")
    end_factor = jnp.where((shard == 0) | (shard == shards - 1), 1.0, 2.0).astype(jnp.float32)
    hessian = period_hessian(selected, line_weight[0, 0], barrier[0, 0], ramp_weight, end_factor)
    link_float = link_columns[0, 0].astype(jnp.float32)
    rhs = jnp.concatenate([gradient[0, 0][:, None], link_float], axis=1)
    h_nn = hessian[count:, count:]
    h_nr = hessian[count:, :count]
    h_rr = hessian[:count, :count]
    l_nn = lax.linalg.cholesky(h_nn)
    solved = trsm(l_nn, jnp.concatenate([h_nr, rhs[count:]], axis=1))
    x_nr = solved[:, :count]
    y_n = solved[:, count:]
    schur = h_rr - jnp.dot(x_nr.T, x_nr, precision=highest)
    reduced = rhs[:count] - jnp.dot(x_nr.T, y_n, precision=highest)
    mine = jnp.concatenate([schur, reduced], axis=1)
    other = lax.ppermute(mine, "tm", [(0, 1), (1, 0)])
    first = shard == 0
    part0 = jnp.where(first, mine, other)
    part1 = jnp.where(first, other, mine)
    coupling = -jnp.diag(ramp_weight)
    system = jnp.concatenate(
        [
            jnp.concatenate([part0[:, :count], coupling], axis=1),
            jnp.concatenate([coupling, part1[:, :count]], axis=1),
        ],
        axis=0,
    )
    lower = lax.linalg.cholesky(system)
    ramp_both = jax.scipy.linalg.cho_solve(
        (lower, True), jnp.concatenate([part0[:, count:], part1[:, count:]], axis=0)
    )
    x_r = jnp.where(first, ramp_both[:count], ramp_both[count:])
    x_n = trsm(l_nn, y_n - jnp.dot(x_nr, x_r, precision=highest), transpose=True)
    solution_cols = jnp.concatenate([x_r, x_n], axis=0)
    step_vec = solution_cols[:, 0]
    step_cols = solution_cols[:, 1:]
    local = jnp.dot(link_float.T, solution_cols, precision=highest)
    total = butterfly_sum(local, ("tm", "scen", "line"))
    vec_total = total[:, 0]
    mat_total = total[:, 1:]
    inverse_count = 1.0 / (shards * lax.axis_size("scen") * lax.axis_size("line"))
    link_system = jnp.diag(link_diag) + inverse_count * mat_total
    right_side = inverse_count * vec_total - link_rhs
    link_lower = jnp.linalg.cholesky(link_system)
    link_step = jax.scipy.linalg.cho_solve((link_lower, True), right_side)
    newton_step = step_vec - jnp.dot(step_cols, link_step, precision=highest)
    return (newton_step[None, None], link_step)


def solution(mesh):
    return jax.shard_map(
        on_device,
        mesh=mesh,
        in_specs=(
            P("line", None, None),
            P(("scen", "line"), "tm", None),
            P(("scen", "line"), "tm", None, None),
            P(("scen", "line"), "tm", None),
            P(("scen", "line"), "tm", None),
            P(("scen", "line"), "tm", None, None),
            P(),
            P(),
            P(),
        ),
        out_specs=(P(("scen", "line"), "tm", None), P()),
        check_vma=False,
    )
```

profile of v0, /device:TPU:2, one launch (start us, length us, event | category | flops | bytes accessed | tf_op | source)
XLA Modules:
  0.0 658.7 jit_solution(9514112737942022669)
XLA Ops:
  12.1 141.1 %all-gather.2.cloned.1.call-done = bf16[64,128,1024]{2,1,0:T(8,128)(2,1)} async-done(((bf16[2,128,1024]{2,1,0:T(8,128)(2,1)}), bf16[64,128,1024]{2,1,0:T(8,128)(2,1)}) %all-gather.2.cloned.1.call-update) | async-done | bytes 16777232 | tf_op jit(solution)/shard_map/all_gather | solution.py:52
  153.3 6.4 gather_fusion
  170.7 11.7 %cholesky.243 = f32[128,128]{1,0:T(8,128)S(1)} custom-call(f32[128,128]{1,0:T(8,128)S(1)} %copy.59), custom_call_target="Cholesky" | custom-call | tf_op jit(solution)/shard_map/cholesky | solution.py:63
  182.5 9.8 %custom-call.59 = f32[1,128,128]{1,2,0:T(8,128)S(1)} custom-call(f32[1,128,128]{2,1,0:T(8,128)S(1)} %get-tuple-element.78), custom_call_target="InvertDiagBlocksLowerTriangular" | custom-call | tf_op jit(solution)/shard_map/cholesky | solution.py:63
  196.3 12.5 %cholesky.266 = f32[128,128]{1,0:T(8,128)S(1)} custom-call(f32[128,128]{1,0:T(8,128)} %copy.61), custom_call_target="Cholesky" | custom-call | tf_op jit(solution)/shard_map/cholesky | solution.py:63
  209.5 10.8 %custom-call.60 = f32[1,128,128]{1,2,0:T(8,128)S(1)} custom-call(f32[1,128,128]{2,1,0:T(8,128)} %get-tuple-element.75), custom_call_target="InvertDiagBlocksLowerTriangular" | custom-call | tf_op jit(solution)/shard_map/cholesky | solution.py:63
  223.3 12.5 %cholesky.293 = f32[128,128]{1,0:T(8,128)S(1)} custom-call(f32[128,128]{1,0:T(8,128)} %copy.63), custom_call_target="Cholesky" | custom-call | tf_op jit(solution)/shard_map/cholesky | solution.py:63
  236.6 9.8 %custom-call.67 = f32[1,128,128]{1,2,0:T(8,128)S(1)} custom-call(f32[1,128,128]{2,1,0:T(8,128)S(1)} %get-tuple-element.72), custom_call_target="InvertDiagBlocksLowerTriangular" | custom-call | tf_op jit(solution)/shard_map/cholesky/custom-call.17 | solution.py:63
  248.6 12.2 %cholesky.522 = f32[128,128]{1,0:T(8,128)S(1)} custom-call(f32[128,128]{1,0:T(8,128)S(1)} %copy.66), custom_call_target="Cholesky" | custom-call | tf_op jit(solution)/shard_map/cholesky | solution.py:63
  261.5 9.8 %custom-call.68 = f32[1,128,128]{1,2,0:T(8,128)S(1)} custom-call(f32[1,128,128]{2,1,0:T(8,128)S(1)} %get-tuple-element.69), custom_call_target="InvertDiagBlocksLowerTriangular" | custom-call | tf_op jit(solution)/shard_map/cholesky/custom-call.18 | solution.py:63
  273.4 11.7 %cholesky.537 = f32[128,128]{1,0:T(8,128)S(1)} custom-call(f32[128,128]{1,0:T(8,128)S(1)} %copy.69), custom_call_target="Cholesky" | custom-call | tf_op jit(solution)/shard_map/cholesky | solution.py:63
  285.8 9.8 %custom-call.69 = f32[1,128,128]{1,2,0:T(8,128)S(1)} custom-call(f32[1,128,128]{2,1,0:T(8,128)S(1)} %get-tuple-element.66), custom_call_target="InvertDiagBlocksLowerTriangular" | custom-call | tf_op jit(solution)/shard_map/cholesky/custom-call.19 | solution.py:63
  297.3 11.9 %cholesky.551 = f32[128,128]{1,0:T(8,128)S(1)} custom-call(f32[128,128]{1,0:T(8,128)S(1)} %copy.72), custom_call_target="Cholesky" | custom-call | tf_op jit(solution)/shard_map/cholesky | solution.py:63
  316.0 21.1 %while.2 = (s32[]{:T(128)}, f32[768,768]{1,0:T(8,128)}, s32[6,2]{0,1:T(2,128)S(1)}, f32[6,128,128]{2,1,0:T(8,128)}, s32[]{:T(128)}) while((s32[]{:T(128)}, f32[768,768]{1,0:T(8,128)}, s32[6,2]{0,1:T(2,128)S(1)}, f32[6,128,128]{2,1,0:T(8,128)}, s32[]{:T(128)}) %tuple.70), condition=%wide.while_cond, body=%wide.while_body.sunk | while | flops 2 | bytes 132705 | solution.py:34
  337.1 59.8 %custom-call.61 = f32[6,128,128]{1,2,0:T(8,128)S(1)} custom-call(f32[6,128,128]{2,1,0:T(8,128)} %get-tuple-element.12), custom_call_target="InvertDiagBlocksLowerTriangular" | custom-call | tf_op jit(solution)/shard_map/triangular_solve | solution.py:34
  418.7 11.7 %cholesky.565 = f32[128,128]{1,0:T(8,128)S(1)} custom-call(f32[128,128]{1,0:T(8,128)S(1)} %cholesky.649), custom_call_target="Cholesky" | custom-call | tf_op jit(solution)/shard_map/cholesky | solution.py:82
  430.6 9.8 %custom-call.70 = f32[1,128,128]{1,2,0:T(8,128)S(1)} custom-call(f32[1,128,128]{2,1,0:T(8,128)S(1)} %get-tuple-element.62), custom_call_target="InvertDiagBlocksLowerTriangular" | custom-call | tf_op jit(solution)/shard_map/cholesky/custom-call.17 | solution.py:82
  442.9 11.7 %cholesky.576 = f32[128,128]{1,0:T(8,128)S(1)} custom-call(f32[128,128]{1,0:T(8,128)S(1)} %cholesky.653), custom_call_target="Cholesky" | custom-call | tf_op jit(solution)/shard_map/cholesky | solution.py:82
  455.9 10.0 %custom-call.71 = f32[1,128,128]{1,2,0:T(8,128)S(1)} custom-call(f32[1,128,128]{2,1,0:T(8,128)S(1)} %get-tuple-element.59), custom_call_target="InvertDiagBlocksLowerTriangular" | custom-call | tf_op jit(solution)/shard_map/cholesky/custom-call.18 | solution.py:82
  467.5 11.7 %cholesky.593 = f32[128,128]{1,0:T(8,128)S(1)} custom-call(f32[128,128]{1,0:T(8,128)S(1)} %cholesky.658), custom_call_target="Cholesky" | custom-call | tf_op jit(solution)/shard_map/cholesky | solution.py:82
  479.8 9.8 %custom-call.72 = f32[1,128,128]{1,2,0:T(8,128)S(1)} custom-call(f32[1,128,128]{2,1,0:T(8,128)S(1)} %get-tuple-element.56), custom_call_target="InvertDiagBlocksLowerTriangular" | custom-call | tf_op jit(solution)/shard_map/cholesky/custom-call.19 | solution.py:82
  491.1 11.9 %cholesky.606 = f32[128,128]{1,0:T(8,128)S(1)} custom-call(f32[128,128]{1,0:T(8,128)S(1)} %convolution_subtract_fusion.23), custom_call_target="Cholesky" | custom-call | tf_op jit(solution)/shard_map/cholesky | solution.py:82
  506.4 10.9 %while.3 = (s32[]{:T(128)}, f32[512,512]{1,0:T(8,128)S(1)}, s32[4,2]{0,1:T(2,128)S(1)}, f32[4,128,128]{2,1,0:T(8,128)}, s32[]{:T(128)}) while((s32[]{:T(128)}, f32[512,512]{1,0:T(8,128)S(1)}, s32[4,2]{0,1:T(2,128)S(1)}, f32[4,128,128]{2,1,0:T(8,128)}, s32[]{:T(128)}) %tuple.73), condition=%wide.while_cond.1, body=%wide.while_body.1.sunk | while | flops 2 | bytes 132705 | solution.py:83
  517.3 40.1 %custom-call.62 = f32[4,128,128]{1,2,0:T(8,128)S(1)} custom-call(f32[4,128,128]{2,1,0:T(8,128)} %get-tuple-element.20), custom_call_target="InvertDiagBlocksLowerTriangular" | custom-call | tf_op jit(solution)/shard_map/jit(_cho_solve)/triangular_solve | solution.py:83
  576.7 5.0 collective-permute-done.2
  588.6 5.1 collective-permute-done.4
  595.2 5.4 collective-permute-done.5
  600.7 5.4 collective-permute-done.6
  608.1 8.2 %collective-permute-done.7 = f32[128,129]{1,0:T(8,128)S(1)} collective-permute-done((f32[128,129]{1,0:T(8,128)S(1)}, f32[128,129]{1,0:T(8,128)S(1)}, u32[]{:S(2)}, u32[]{:S(2)}) %collective-permute-start.7) | collective-permute-done | bytes 66080 | tf_op jit(solution)/shard_map/ppermute | solution.py:28
  620.1 6.6 %collective-permute-done.8 = f32[128,129]{1,0:T(8,128)S(1)} collective-permute-done((f32[128,129]{1,0:T(8,128)S(1)}, f32[128,129]{1,0:T(8,128)S(1)}, u32[]{:S(2)}, u32[]{:S(2)}) %collective-permute-start.8) | collective-permute-done | bytes 66080 | tf_op jit(solution)/shard_map/ppermute | solution.py:28
  627.2 11.7 %cholesky.617 = f32[128,128]{1,0:T(8,128)S(1)} custom-call(f32[128,128]{1,0:T(8,128)S(1)} %fusion.125), custom_call_target="Cholesky" | custom-call | tf_op jit(solution)/shard_map/jit(cholesky)/cholesky | solution.py:98
  640.2 9.8 %custom-call.63 = f32[1,128,128]{1,2,0:T(8,128)S(1)} custom-call(f32[1,128,128]{2,1,0:T(8,128)S(1)} %fusion.110), custom_call_target="InvertDiagBlocksLowerTriangular" | custom-call | tf_op jit(solution)/shard_map/jit(_cho_solve)/triangular_solve | solution.py:99
  (238 shorter events, 132.8 us)
Async XLA Ops:
  7.2 4.9 copy-start.21
  7.2 4.9 copy-start.15
  7.2 4.9 copy-start.16
  7.2 146.1 %all-gather.2.cloned.1.call-start = ((), (), s32[]{:S(2)}) async-start(), calls=%async_computation | async-start | bytes 17301504 | tf_op jit(solution)/shard_map/all_gather | solution.py:52
  9.8 0.8 copy-start.3
  10.6 149.1 %copy-start.20 = (f32[1,1,8,128]{3,2,1,0:T(8,128)S(1)}, f32[1,1,8,128]{3,2,1,0:T(8,128)}, u32[]{:S(2)}) copy-start(f32[1,1,8,128]{3,2,1,0:T(8,128)} %param.17) | copy-start | bytes 12292
  162.3 2.6 copy-start.1
  169.2 1.4 copy-start.2
  316.0 82.3 %copy-start = (f32[768,129]{0,1:T(8,128)S(1)}, f32[768,129]{0,1:T(8,128)}, u32[]{:S(2)}) copy-start(f32[768,129]{0,1:T(8,128)} %fusion.34) | copy-start | bytes 1188868
  396.9 11.7 %copy-start.11 = (f32[6,128,128]{1,2,0:T(8,128)}, f32[6,128,128]{1,2,0:T(8,128)S(1)}, u32[]{:S(2)}) copy-start(f32[6,128,128]{1,2,0:T(8,128)S(1)} %custom-call.61) | copy-start | bytes 1179652
  406.4 4.4 copy-start.4
  406.4 4.4 copy-start.14
  411.9 2.2 collective-permute-start
  412.4 2.7 copy-start.6
  414.1 0.8 copy-start.9
  414.2 0.9 copy-start.10
  414.2 1.0 copy-start.7
  415.2 0.7 copy-start.8
  417.7 1.0 copy-start.5
  561.5 4.3 copy-start.12
  567.2 6.9 %copy-start.13 = (bf16[1,1,1024,128]{3,2,1,0:T(8,128)(2,1)S(1)}, bf16[1,1,1024,128]{3,2,1,0:T(8,128)(2,1)}, u32[]{:S(2)}) copy-start(bf16[1,1,1024,128]{3,2,1,0:T(8,128)(2,1)} %param.20) | copy-start | bytes 786436
  574.0 52.8 %copy-start.17 = (f32[128]{0:T(128)S(1)}, f32[128]{0:T(128)}, u32[]{:S(2)}) copy-start(f32[128]{0:T(128)} %param.22) | copy-start | bytes 1540
  574.1 75.9 %copy-start.19 = (f32[128]{0:T(128)S(1)}, f32[128]{0:T(128)}, u32[]{:S(2)}) copy-start(f32[128]{0:T(128)} %param.23) | copy-start | bytes 1540
  574.6 1.4 collective-permute-start.1
  576.1 5.6 collective-permute-start.2
  581.7 6.6 collective-permute-start.3
  588.3 5.4 collective-permute-start.4
  593.8 6.8 %collective-permute-start.5 = (f32[128,129]{1,0:T(8,128)S(1)}, f32[128,129]{1,0:T(8,128)S(1)}, u32[]{:S(2)}, u32[]{:S(2)}) collective-permute-start(f32[128,129]{1,0:T(8,128)S(1)} %add.143), channel_id=1, source_target_pairs={{0,2},{1,3},{2,0},{3,1},{4,6},{5,7},{6,4},{7,5},{8,10},{9,11},{10,... | collective-permute-start | bytes 198152 | tf_op jit(solution)/shard_map/ppermute | solution.py:28
  600.6 5.5 collective-permute-start.6
  606.1 10.2 %collective-permute-start.7 = (f32[128,129]{1,0:T(8,128)S(1)}, f32[128,129]{1,0:T(8,128)S(1)}, u32[]{:S(2)}, u32[]{:S(2)}) collective-permute-start(f32[128,129]{1,0:T(8,128)S(1)} %add.145), channel_id=1, source_target_pairs={{0,8},{1,9},{2,10},{3,11},{4,12},{5,13},{6,14},{7,15},{8,0},{9,1},... | collective-permute-start | bytes 198152 | tf_op jit(solution)/shard_map/ppermute | solution.py:28
  616.3 10.4 %collective-permute-start.8 = (f32[128,129]{1,0:T(8,128)S(1)}, f32[128,129]{1,0:T(8,128)S(1)}, u32[]{:S(2)}, u32[]{:S(2)}) collective-permute-start(f32[128,129]{1,0:T(8,128)S(1)} %add.146), channel_id=1, source_target_pairs={{0,16},{1,17},{2,18},{3,19},{4,20},{5,21},{6,22},{7,23},{8,24},{9,... | collective-permute-start | bytes 198152 | tf_op jit(solution)/shard_map/ppermute | solution.py:28
  650.4 1.1 copy-start.18
Sparse Core Ops, SparseCore 0:
  10.6 142.6 all-gather.1
where the time goes:
time: 664 us; the launch traced here: 659 us
  other arithmetic  337 us (51%)
  waiting for transfers between devices  185 us (28%)
  local copies, waits for them, and re-layouts  51.9 us (8%)
  matrix products  51.5 us (8%)
  between operations  21.9 us (3%)
  starting transfers between devices  11.1 us (2%)
    all_gather x1, waiting for transfers between devices, on_device(): every_block = lax.all_gather(line_blocks, 'line', axis=0, tiled=True)  141 us
    another operation x22, other arithmetic, on_device(): l_nn = lax.linalg.cholesky(h_nn)  127 us
    another operation x15, other arithmetic, on_device(): lower = lax.linalg.cholesky(system)  79.4 us
    another operation x3, other arithmetic, trsm(): lax.linalg.triangular_solve(a, b, left_side=True, lower=True, transpose_a...  61.4 us
    ppermute x8, waiting for transfers between devices, butterfly_sum(): value = value + lax.ppermute(value, axis, pairs)  41.3 us
    another operation x3, other arithmetic, on_device(): jax.scipy.linalg.cho_solve((lower, True), jnp.concatenate([part0[:, count...  40.3 us
    another operation x30, local copies, waits for them, and re-layouts  32 us
    another operation x22, matrix products, trsm(): lax.linalg.triangular_solve(a, b, left_side=True, lower=True, transpose_a...  20.2 us
  transfers between devices with their start and end apart: 10, of which 10 were waited for; matrix products, arithmetic and copies ran while one was open for 1% of the time, Pallas kernels for 0%

commit v1 on v0

--- a/solution.py
+++ b/solution.py
@@ -49,7 +49,9 @@
     order = line_blocks.shape[2]
     count = ramp_weight.shape[0]
     links = link_columns.shape[-1]
-    every_block = lax.all_gather(line_blocks, "line", axis=0, tiled=True)
+    every_block = jnp.concatenate(
+        lax.all_to_all(jnp.stack([line_blocks] * lax.axis_size("line")), "line", 0, 0), axis=0
+    )
     selected = jnp.take(every_block, block_ids, axis=0)
     shard = lax.axis_index("tm")
     shards = lax.axis_size("tm")

time: 664 us -> 929 us (1.40)
  waiting for transfers between devices: 185 us -> 420 us
  starting transfers between devices: 11.1 us -> 47 us
  between operations: 21.9 us -> 8.53 us
    all_to_all x0 -> x1, waiting for transfers between devices: none -> 379 us  [on_device(): lax.all_to_all(jnp.stack([line_blocks] * lax.axis_size('line')), 'line',...]
    all_gather x1 -> x0, waiting for transfers between devices: 141 us -> none  [on_device(): every_block = lax.all_gather(line_blocks, 'line', axis=0, tiled=True)]
    ppermute x8, starting transfers between devices: 10.6 us -> 34.8 us  [butterfly_sum(): value = value + lax.ppermute(value, axis, pairs)]
    all_to_all x0 -> x1, starting transfers between devices: none -> 11.8 us  [on_device(): lax.all_to_all(jnp.stack([line_blocks] * lax.axis_size('line')), 'line',...]
    another operation x30 -> x31, local copies, waits for them, and re-layouts: 32 us -> 38.8 us
  transfers between devices with their start and end apart: 10 -> 10, of which waited for: 10 -> 10; matrix products, arithmetic and copies ran while one was open for 1% -> 0% of each run, Pallas kernels for 0% -> 0%
where the time goes in v1:
time: 929 us; the launch traced here: 922 us
  waiting for transfers between devices  420 us (45%)
  other arithmetic  337 us (36%)
  local copies, waits for them, and re-layouts  58.1 us (6%)
  matrix products  51.6 us (6%)
  starting transfers between devices  47 us (5%)
    all_to_all x1, waiting for transfers between devices, on_device(): lax.all_to_all(jnp.stack([line_blocks] * lax.axis_size('line')), 'line',...  379 us
    another operation x22, other arithmetic, on_device(): l_nn = lax.linalg.cholesky(h_nn)  127 us
    another operation x15, other arithmetic, on_device(): lower = lax.linalg.cholesky(system)  79.4 us
    another operation x3, other arithmetic, trsm(): lax.linalg.triangular_solve(a, b, left_side=True, lower=True, transpose_a...  61.9 us
    another operation x3, other arithmetic, on_device(): jax.scipy.linalg.cho_solve((lower, True), jnp.concatenate([part0[:, count...  40.3 us
    ppermute x8, waiting for transfers between devices, butterfly_sum(): value = value + lax.ppermute(value, axis, pairs)  39.3 us
    ppermute x8, starting transfers between devices, butterfly_sum(): value = value + lax.ppermute(value, axis, pairs)  34.8 us
    another operation x30, local copies, waits for them, and re-layouts  31.9 us
  transfers between devices with their start and end apart: 10, of which 10 were waited for; matrix products, arithmetic and copies ran while one was open for 0% of the time, Pallas kernels for 0%

profile of v1, /device:TPU:2, one launch (start us, length us, event | category | flops | bytes accessed | tf_op | source)
XLA Modules:
  0.0 922.3 jit_solution(1349521557896544419)
XLA Ops:
  0.6 6.8 stack.2
  7.5 11.8 %all-to-all-start = ((bf16[32,2,128,1024]{3,2,1,0:T(8,128)(2,1)}), bf16[32,2,128,1024]{3,2,1,0:T(8,128)(2,1)}, u32[]{:S(2)}, u32[]{:S(2)}) async-start(bf16[32,2,128,1024]{3,2,1,0:T(8,128)(2,1)} %stack.2), calls=%async_computation | async-start | bytes 33554432 | tf_op jit(solution)/shard_map/all_to_all | solution.py:53
  21.7 379.5 %all-to-all-done = bf16[32,2,128,1024]{3,2,1,0:T(8,128)(2,1)} async-done(((bf16[32,2,128,1024]{3,2,1,0:T(8,128)(2,1)}), bf16[32,2,128,1024]{3,2,1,0:T(8,128)(2,1)}, u32[]{:S(2)}, u32[]{:S(2)}) %all-to-all-start) | async-done | bytes 16777248 | tf_op jit(solution)/shard_map/all_to_all | solution.py:53
  401.2 6.4 gather_fusion
  419.0 11.7 %cholesky.243 = f32[128,128]{1,0:T(8,128)S(1)} custom-call(f32[128,128]{1,0:T(8,128)S(1)} %copy.36), custom_call_target="Cholesky" | custom-call | tf_op jit(solution)/shard_map/cholesky | solution.py:65
  430.8 9.8 %custom-call.59 = f32[1,128,128]{1,2,0:T(8,128)S(1)} custom-call(f32[1,128,128]{2,1,0:T(8,128)S(1)} %get-tuple-element.78), custom_call_target="InvertDiagBlocksLowerTriangular" | custom-call | tf_op jit(solution)/shard_map/cholesky | solution.py:65
  444.6 12.5 %cholesky.266 = f32[128,128]{1,0:T(8,128)S(1)} custom-call(f32[128,128]{1,0:T(8,128)} %copy.38), custom_call_target="Cholesky" | custom-call | tf_op jit(solution)/shard_map/cholesky | solution.py:65
  457.8 10.8 %custom-call.60 = f32[1,128,128]{1,2,0:T(8,128)S(1)} custom-call(f32[1,128,128]{2,1,0:T(8,128)} %get-tuple-element.75), custom_call_target="InvertDiagBlocksLowerTriangular" | custom-call | tf_op jit(solution)/shard_map/cholesky | solution.py:65
  471.5 12.5 %cholesky.293 = f32[128,128]{1,0:T(8,128)S(1)} custom-call(f32[128,128]{1,0:T(8,128)} %copy.40), custom_call_target="Cholesky" | custom-call | tf_op jit(solution)/shard_map/cholesky | solution.py:65
  484.8 9.8 %custom-call.67 = f32[1,128,128]{1,2,0:T(8,128)S(1)} custom-call(f32[1,128,128]{2,1,0:T(8,128)S(1)} %get-tuple-element.72), custom_call_target="InvertDiagBlocksLowerTriangular" | custom-call | tf_op jit(solution)/shard_map/cholesky/custom-call.17 | solution.py:65
  496.9 12.1 %cholesky.522 = f32[128,128]{1,0:T(8,128)S(1)} custom-call(f32[128,128]{1,0:T(8,128)S(1)} %copy.43), custom_call_target="Cholesky" | custom-call | tf_op jit(solution)/shard_map/cholesky | solution.py:65
  509.7 9.8 %custom-call.68 = f32[1,128,128]{1,2,0:T(8,128)S(1)} custom-call(f32[1,128,128]{2,1,0:T(8,128)S(1)} %get-tuple-element.69), custom_call_target="InvertDiagBlocksLowerTriangular" | custom-call | tf_op jit(solution)/shard_map/cholesky/custom-call.18 | solution.py:65
  521.6 11.7 %cholesky.537 = f32[128,128]{1,0:T(8,128)S(1)} custom-call(f32[128,128]{1,0:T(8,128)S(1)} %copy.46), custom_call_target="Cholesky" | custom-call | tf_op jit(solution)/shard_map/cholesky | solution.py:65
  534.0 9.8 %custom-call.69 = f32[1,128,128]{1,2,0:T(8,128)S(1)} custom-call(f32[1,128,128]{2,1,0:T(8,128)S(1)} %get-tuple-element.66), custom_call_target="InvertDiagBlocksLowerTriangular" | custom-call | tf_op jit(solution)/shard_map/cholesky/custom-call.19 | solution.py:65
  545.5 11.9 %cholesky.551 = f32[128,128]{1,0:T(8,128)S(1)} custom-call(f32[128,128]{1,0:T(8,128)S(1)} %copy.49), custom_call_target="Cholesky" | custom-call | tf_op jit(solution)/shard_map/cholesky | solution.py:65
  564.2 21.1 %while.2 = (s32[]{:T(128)}, f32[768,768]{1,0:T(8,128)}, s32[6,2]{0,1:T(2,128)S(1)}, f32[6,128,128]{2,1,0:T(8,128)}, s32[]{:T(128)}) while((s32[]{:T(128)}, f32[768,768]{1,0:T(8,128)}, s32[6,2]{0,1:T(2,128)S(1)}, f32[6,128,128]{2,1,0:T(8,128)}, s32[]{:T(128)}) %tuple.70), condition=%wide.while_cond, body=%wide.while_body.sunk | while | flops 2 | bytes 132705 | solution.py:34
  585.3 59.8 %custom-call.61 = f32[6,128,128]{1,2,0:T(8,128)S(1)} custom-call(f32[6,128,128]{2,1,0:T(8,128)} %get-tuple-element.12), custom_call_target="InvertDiagBlocksLowerTriangular" | custom-call | tf_op jit(solution)/shard_map/triangular_solve | solution.py:34
  666.8 11.7 %cholesky.565 = f32[128,128]{1,0:T(8,128)S(1)} custom-call(f32[128,128]{1,0:T(8,128)S(1)} %cholesky.649), custom_call_target="Cholesky" | custom-call | tf_op jit(solution)/shard_map/cholesky | solution.py:84
  678.7 9.8 %custom-call.70 = f32[1,128,128]{1,2,0:T(8,128)S(1)} custom-call(f32[1,128,128]{2,1,0:T(8,128)S(1)} %get-tuple-element.62), custom_call_target="InvertDiagBlocksLowerTriangular" | custom-call | tf_op jit(solution)/shard_map/cholesky/custom-call.17 | solution.py:84
  691.1 11.7 %cholesky.576 = f32[128,128]{1,0:T(8,128)S(1)} custom-call(f32[128,128]{1,0:T(8,128)S(1)} %cholesky.653), custom_call_target="Cholesky" | custom-call | tf_op jit(solution)/shard_map/cholesky | solution.py:84
  704.1 10.0 %custom-call.71 = f32[1,128,128]{1,2,0:T(8,128)S(1)} custom-call(f32[1,128,128]{2,1,0:T(8,128)S(1)} %get-tuple-element.59), custom_call_target="InvertDiagBlocksLowerTriangular" | custom-call | tf_op jit(solution)/shard_map/cholesky/custom-call.18 | solution.py:84
  715.6 11.7 %cholesky.593 = f32[128,128]{1,0:T(8,128)S(1)} custom-call(f32[128,128]{1,0:T(8,128)S(1)} %cholesky.658), custom_call_target="Cholesky" | custom-call | tf_op jit(solution)/shard_map/cholesky | solution.py:84
  728.0 9.8 %custom-call.72 = f32[1,128,128]{1,2,0:T(8,128)S(1)} custom-call(f32[1,128,128]{2,1,0:T(8,128)S(1)} %get-tuple-element.56), custom_call_target="InvertDiagBlocksLowerTriangular" | custom-call | tf_op jit(solution)/shard_map/cholesky/custom-call.19 | solution.py:84
  739.2 11.9 %cholesky.606 = f32[128,128]{1,0:T(8,128)S(1)} custom-call(f32[128,128]{1,0:T(8,128)S(1)} %convolution_subtract_fusion.23), custom_call_target="Cholesky" | custom-call | tf_op jit(solution)/shard_map/cholesky | solution.py:84
  754.5 10.9 %while.3 = (s32[]{:T(128)}, f32[512,512]{1,0:T(8,128)S(1)}, s32[4,2]{0,1:T(2,128)S(1)}, f32[4,128,128]{2,1,0:T(8,128)}, s32[]{:T(128)}) while((s32[]{:T(128)}, f32[512,512]{1,0:T(8,128)S(1)}, s32[4,2]{0,1:T(2,128)S(1)}, f32[4,128,128]{2,1,0:T(8,128)}, s32[]{:T(128)}) %tuple.73), condition=%wide.while_cond.1, body=%wide.while_body.1.sunk | while | flops 2 | bytes 132705 | solution.py:85
  765.4 40.1 %custom-call.62 = f32[4,128,128]{1,2,0:T(8,128)S(1)} custom-call(f32[4,128,128]{2,1,0:T(8,128)} %get-tuple-element.20), custom_call_target="InvertDiagBlocksLowerTriangular" | custom-call | tf_op jit(solution)/shard_map/jit(_cho_solve)/triangular_solve | solution.py:85
  843.1 27.9 %collective-permute-start.5 = (f32[128,129]{1,0:T(8,128)S(1)}, f32[128,129]{1,0:T(8,128)S(1)}, u32[]{:S(2)}, u32[]{:S(2)}) collective-permute-start(f32[128,129]{1,0:T(8,128)S(1)} %add.143), channel_id=1, source_target_pairs={{0,2},{1,3},{2,0},{3,1},{4,6},{5,7},{6,4},{7,5},{8,10},{9,11},{10,... | collective-permute-start | bytes 198152 | tf_op jit(solution)/shard_map/ppermute | solution.py:28
  874.1 6.3 collective-permute-done.6
  880.5 7.6 collective-permute-done.7
  888.3 8.8 collective-permute-done.8
  897.6 11.7 %cholesky.617 = f32[128,128]{1,0:T(8,128)S(1)} custom-call(f32[128,128]{1,0:T(8,128)S(1)} %fusion.125), custom_call_target="Cholesky" | custom-call | tf_op jit(solution)/shard_map/jit(cholesky)/cholesky | solution.py:100
  910.6 9.8 %custom-call.63 = f32[1,128,128]{1,2,0:T(8,128)S(1)} custom-call(f32[1,128,128]{2,1,0:T(8,128)S(1)} %fusion.110), custom_call_target="InvertDiagBlocksLowerTriangular" | custom-call | tf_op jit(solution)/shard_map/jit(_cho_solve)/triangular_solve | solution.py:101
  (242 shorter events, 138.1 us)
Async XLA Ops:
  7.4 11.8 %copy-start.13 = (bf16[1,1,1024,128]{3,2,1,0:T(8,128)(2,1)S(1)}, bf16[1,1,1024,128]{3,2,1,0:T(8,128)(2,1)}, u32[]{:S(2)}) copy-start(bf16[1,1,1024,128]{3,2,1,0:T(8,128)(2,1)} %param.20) | copy-start | bytes 786436
  7.4 12.6 %copy-start.22 = (s32[1,1,8]{2,1,0:T(1,128)S(1)}, s32[1,1,8]{2,1,0:T(1,128)}, u32[]{:S(2)}) copy-start(s32[1,1,8]{2,1,0:T(1,128)} %param.16) | copy-start | bytes 100
  7.4 13.4 %copy-start.15 = (f32[1,1,1024]{2,1,0:T(1,128)S(1)}, f32[1,1,1024]{2,1,0:T(1,128)}, u32[]{:S(2)}) copy-start(f32[1,1,1024]{2,1,0:T(1,128)} %param.19) | copy-start | bytes 12292
  7.4 14.2 %copy-start.16 = (f32[256]{0:T(256)S(1)}, f32[256]{0:T(256)}, u32[]{:S(2)}) copy-start(f32[256]{0:T(256)} %param.21) | copy-start | bytes 3076
  7.5 14.2 %copy-start.17 = (f32[1,1,1024]{2,1,0:T(1,128)S(1)}, f32[1,1,1024]{2,1,0:T(1,128)}, u32[]{:S(2)}) copy-start(f32[1,1,1024]{2,1,0:T(1,128)} %param.18) | copy-start | bytes 12292
  7.5 393.7 %all-to-all-start = ((bf16[32,2,128,1024]{3,2,1,0:T(8,128)(2,1)}), bf16[32,2,128,1024]{3,2,1,0:T(8,128)(2,1)}, u32[]{:S(2)}, u32[]{:S(2)}) async-start(bf16[32,2,128,1024]{3,2,1,0:T(8,128)(2,1)} %stack.2), calls=%async_computation | async-start | bytes 33554432 | tf_op jit(solution)/shard_map/all_to_all | solution.py:53
  20.1 0.8 copy-start.3
  20.9 386.8 %copy-start.21 = (f32[1,1,8,128]{3,2,1,0:T(8,128)S(1)}, f32[1,1,8,128]{3,2,1,0:T(8,128)}, u32[]{:S(2)}) copy-start(f32[1,1,8,128]{3,2,1,0:T(8,128)} %param.17) | copy-start | bytes 12292
  410.3 2.6 copy-start.1
  417.5 1.4 copy-start.2
  562.5 1.6 copy-start.23
  564.2 82.3 %copy-start = (f32[768,129]{0,1:T(8,128)S(1)}, f32[768,129]{0,1:T(8,128)}, u32[]{:S(2)}) copy-start(f32[768,129]{0,1:T(8,128)} %fusion.34) | copy-start | bytes 1188868
  645.0 11.7 %copy-start.11 = (f32[6,128,128]{1,2,0:T(8,128)}, f32[6,128,128]{1,2,0:T(8,128)S(1)}, u32[]{:S(2)}) copy-start(f32[6,128,128]{1,2,0:T(8,128)S(1)} %custom-call.61) | copy-start | bytes 1179652
  654.6 4.4 copy-start.4
  660.0 2.2 collective-permute-start
  660.6 2.7 copy-start.6
  662.3 0.9 copy-start.10
  662.3 1.0 copy-start.7
  665.8 1.0 copy-start.5
  809.6 4.5 copy-start.12
  815.5 6.9 copy-start.14
  822.3 74.9 %copy-start.18 = (f32[128]{0:T(128)S(1)}, f32[128]{0:T(128)}, u32[]{:S(2)}) copy-start(f32[128]{0:T(128)} %param.22) | copy-start | bytes 1540
  822.4 98.0 %copy-start.20 = (f32[128]{0:T(128)S(1)}, f32[128]{0:T(128)}, u32[]{:S(2)}) copy-start(f32[128]{0:T(128)} %param.23) | copy-start | bytes 1540
  822.9 1.4 collective-permute-start.1
  824.4 5.6 collective-permute-start.2
  830.0 6.6 collective-permute-start.3
  836.6 6.5 collective-permute-start.4
  843.1 30.8 %collective-permute-start.5 = (f32[128,129]{1,0:T(8,128)S(1)}, f32[128,129]{1,0:T(8,128)S(1)}, u32[]{:S(2)}, u32[]{:S(2)}) collective-permute-start(f32[128,129]{1,0:T(8,128)S(1)} %add.143), channel_id=1, source_target_pairs={{0,2},{1,3},{2,0},{3,1},{4,6},{5,7},{6,4},{7,5},{8,10},{9,11},{10,... | collective-permute-start | bytes 198152 | tf_op jit(solution)/shard_map/ppermute | solution.py:28
  874.0 6.4 collective-permute-start.6
  880.4 7.7 collective-permute-start.7
  888.2 9.0 collective-permute-start.8
  920.8 1.1 copy-start.19
  (2 other events, 1.5 us)
